TPU v7x, 32 devices: a whole 2x2x4 slice. The times are simulated.
32 devices in a mesh: fsdp: 8 (over y, x, core), dp: 4 (over z).
Axes of the slice: x: 2, y: 2, z: 4, core: 2. Of those that a mesh axis runs over, the one named last changes fastest.
Arguments:
- tokens: bfloat16 [12288, 8192], P(('fsdp', 'dp')), may hold values from -6 to 6
- output_gradient: bfloat16 [12288, 1024], P(('fsdp', 'dp')), may hold values from -6 to 6
- frozen_value_weight: bfloat16 [8192, 1024], P('fsdp'), may hold values from -0.0625 to 0.0625
- adapter_down_maps: bfloat16 [32, 16, 8192], P(('fsdp', 'dp')), may hold values from -0.0625 to 0.0625
- adapter_up_maps: bfloat16 [32, 16, 1024], P(('fsdp', 'dp')), may hold values from -1.5 to 1.5
- block_tenant_ids: int32 [96], P(('fsdp', 'dp')), may hold values from 0 to 31, as said below
- block_live_rows: int32 [96], P(('fsdp', 'dp')), may hold values from 33 to 128, as said below
- tenant_owner_slot: int32 [32], replicated, may hold values from 0 to 31, as said below
Outputs:
- output: bfloat16 [12288, 1024], P(('fsdp', 'dp'))
- token_gradient: bfloat16 [12288, 8192], P(('fsdp', 'dp'))
- grad_down: bfloat16 [32, 16, 8192], P(('fsdp', 'dp'))
- grad_up: bfloat16 [32, 16, 1024], P(('fsdp', 'dp'))
Inputs may be any that keep to these rules, and one draw needn't show every extreme that they name: `block_tenant_ids`: A block held by a device whose index along dp is d names a tenant t with tenant_owner_slot[t] mod (size of dp) = d; tenant_owner_slot is a permutation. `block_live_rows`: the first block of every device is full. `tenant_owner_slot`: each slot is named once.
All inputs are finite; a program needn't handle non-finite values.
Results may differ from a plain program's by a relative error of at most 0.01.
Values may be sent and summed in bfloat16 or wider, within the bound.
No kernel may reach another device: no remote copies, remote signals or barrier semaphores. Data moves between devices by JAX's collectives and lax.ppermute only.
A program may use at most 192 MiB of HBM per device.

v0:
```python
import jax
import jax.numpy as jnp
from jax import lax
from jax.sharding import PartitionSpec as P

ADAPTER_SCALE = 2.0


def on_device(
    tokens,
    output_gradient,
    frozen_value_weight,
    adapter_down_maps,
    adapter_up_maps,
    block_tenant_ids,
    block_live_rows,
    tenant_owner_slot,
):
    tok_rows = tokens.shape[0]
    model_width_size = tokens.shape[1]
    value_width_size = output_gradient.shape[1]
    adapter_rank_size = adapter_down_maps.shape[1]
    number_of_blocks = block_tenant_ids.shape[0]
    block_length = tok_rows // number_of_blocks
    groups = lax.axis_size("dp")
    members = lax.axis_size("fsdp")
    tenant_ids = jnp.arange(tenant_owner_slot.shape[0], dtype=jnp.int32)
    slot_ids = jnp.sum(
        jnp.where(block_tenant_ids[:, None] == tenant_ids[None, :], tenant_owner_slot[None, :], 0),
        axis=1,
    )
    member_ids = slot_ids // groups
    live_rows = (jnp.arange(block_length)[None, :] < block_live_rows[:, None]).astype(jnp.float32)
    live_column = live_rows[:, :, None]
    down_all, up_all = (
        lax.all_gather(adapter_down_maps, "fsdp", axis=0, tiled=True),
        lax.all_gather(adapter_up_maps, "fsdp", axis=0, tiled=True),
    )
    onehot = (member_ids[:, None] == jnp.arange(members)[None, :]).astype(jnp.bfloat16)
    down_block = jnp.dot(onehot, down_all.reshape(members, -1), preferred_element_type=jnp.float32)
    down_block = down_block.astype(jnp.bfloat16).reshape(
        number_of_blocks, adapter_rank_size, model_width_size
    )
    up_block = jnp.dot(onehot, up_all.reshape(members, -1), preferred_element_type=jnp.float32)
    up_block = up_block.astype(jnp.bfloat16).reshape(
        number_of_blocks, adapter_rank_size, value_width_size
    )
    token_blocks = tokens.reshape(number_of_blocks, block_length, model_width_size)
    cot_blocks = output_gradient.reshape(number_of_blocks, block_length, value_width_size)
    low_rank_state = (
        jnp.einsum("cvj,coj->cvo", token_blocks, down_block, preferred_element_type=jnp.float32)
        * live_column
    ).astype(jnp.bfloat16)
    low_rank_gradient = (
        ADAPTER_SCALE
        * jnp.einsum("btv,bkv->btk", cot_blocks, up_block, preferred_element_type=jnp.float32)
        * live_column
    ).astype(jnp.bfloat16)
    adapter_output = jnp.einsum(
        "znr,zrm->znm", low_rank_state, up_block, preferred_element_type=jnp.float32
    )
    adapter_backward = jnp.einsum(
        "uio,uof->uif", low_rank_gradient, down_block, preferred_element_type=jnp.float32
    )
    weight_piece = lax.all_gather(frozen_value_weight, "fsdp", axis=0, tiled=True)
    output_total = jnp.dot(tokens, weight_piece, preferred_element_type=jnp.float32)
    backward_piece = lax.dot_general(
        output_gradient, weight_piece, (((1,), (1,)), ((), ())), preferred_element_type=jnp.float32
    )
    output = live_column * (
        output_total.reshape(number_of_blocks, block_length, value_width_size)
        + ADAPTER_SCALE * adapter_output
    )
    output = output.astype(jnp.bfloat16).reshape(tok_rows, value_width_size)
    token_gradient = live_column * (
        backward_piece.reshape(number_of_blocks, block_length, model_width_size) + adapter_backward
    )
    token_gradient = token_gradient.astype(jnp.bfloat16).reshape(tok_rows, model_width_size)
    partial_down = jnp.einsum(
        "vio,vih->voh", low_rank_gradient, token_blocks, preferred_element_type=jnp.float32
    )
    partial_up = ADAPTER_SCALE * jnp.einsum(
        "btk,btv->bkv", low_rank_state, cot_blocks, preferred_element_type=jnp.float32
    )
    member_range = jnp.arange(members, dtype=jnp.int32)
    table_down = jnp.zeros((members, adapter_rank_size, model_width_size), jnp.float32)
    table_up = jnp.zeros((members, adapter_rank_size, value_width_size), jnp.float32)
    for block_num in range(number_of_blocks):
        picked = (member_range == member_ids[block_num]).astype(jnp.float32)[:, None, None]
        table_down = table_down + picked * partial_down[block_num][None]
        table_up = table_up + picked * partial_up[block_num][None]
    term_down = table_down.astype(jnp.bfloat16)
    term_up = table_up.astype(jnp.bfloat16)
    sum_down, sum_up = (
        lax.psum_scatter(
            term_down.astype(jnp.float32).astype(jnp.bfloat16),
            "fsdp",
            scatter_dimension=0,
            tiled=True,
        ).astype(jnp.float32),
        lax.psum_scatter(
            term_up.astype(jnp.float32).astype(jnp.bfloat16),
            "fsdp",
            scatter_dimension=0,
            tiled=True,
        ).astype(jnp.float32),
    )
    return (output, token_gradient, sum_down.astype(jnp.bfloat16), sum_up.astype(jnp.bfloat16))


def solution(mesh):
    placed = (
        P(("fsdp", "dp"), None),
        P(("fsdp", "dp"), None),
        P("fsdp", None),
        P(("fsdp", "dp"), None, None),
        P(("fsdp", "dp"), None, None),
        P(("fsdp", "dp")),
        P(("fsdp", "dp")),
        P(),
    )
    return jax.shard_map(
        on_device,
        mesh=mesh,
        in_specs=placed,
        out_specs=(
            P(("fsdp", "dp"), None),
            P(("fsdp", "dp"), None),
            P(("fsdp", "dp"), None, None),
            P(("fsdp", "dp"), None, None),
        ),
        check_vma=False,
    )
```

profile of v0, /device:TPU:0, one launch (start us, length us, event | category | flops | bytes accessed | tf_op | source)
XLA Modules:
  0.0 221.4 jit_solution(15387211955821967845)
XLA Ops:
  7.2 0.7 all-gather.5.cloned.1.call-update
  8.0 0.7 all-gather.3.cloned.1.call-update
  8.7 11.0 %all_gather.11 = bf16[8,16,1024]{2,1,0:T(8,128)(2,1)S(1)} all-gather(bf16[1,16,1024]{2,1,0:T(8,128)(2,1)} %param.12), channel_id=1, replica_groups=mesh['fsdp'=8,'dp'=4] {'fsdp'}, dimensions={0}, use_global_device_ids=true | all-gather | bytes 294912 | tf_op jit(solution)/shard_map/all_gather | solution.py:37
  19.8 0.9 select_reduce_fusion
  20.7 0.6 fusion.14
  21.3 0.6 compare_convert_fusion.2
  22.0 1.3 compare_convert_fusion
  23.3 0.7 fusion.10
  24.0 0.3 convolution_convert_fusion.1
  24.3 0.3 fusion.1
  24.6 3.7 %fusion.17 = f32[3,16,8192]{2,1,0:T(8,128)S(1)} fusion(bf16[3,16,128]{2,1,0:T(8,128)(2,1)S(1)} %fusion.1, bf16[3,128,8192]{2,1,0:T(8,128)(2,1)} %bitcast.53), kind=kOutput, calls=%fused_computation.43 | convolution fusion | flops 100663296 | bytes 7876608 | tf_op jit(solution)/shard_map/vio,vih->voh/dot_general | solution.py:79
  28.4 2.2 add_convert_fusion
  30.9 9.6 %all-gather.5.cloned.1.call-done = bf16[8,16,8192]{2,1,0:T(8,128)(2,1)} async-done(((bf16[1,16,8192]{2,1,0:T(8,128)(2,1)}), bf16[8,16,8192]{2,1,0:T(8,128)(2,1)}) %all-gather.5.cloned.1.call-update) | async-done | bytes 2097168 | tf_op jit(solution)/shard_map/all_gather | solution.py:36
  40.5 2.7 %copy.12 = bf16[1,8,16,8192]{3,1,2,0:T(8,128)(2,1)S(1)} copy(bf16[1,8,16,8192]{3,2,1,0:T(8,128)(2,1)} %bitcast.60) | data formatting | bytes 4194304
  43.3 0.8 convolution_convert_fusion
  44.0 4.5 %fusion = bf16[3,16,128]{2,1,0:T(8,128)(2,1)S(1)} fusion(bf16[3,128,8192]{2,1,0:T(8,128)(2,1)} %bitcast.54, bf16[1,3,16,8192]{3,1,2,0:T(4,128)(2,1)S(1)} %bitcast.57, f32[3,128]{1,0:T(4,128)S(1)} %fusion.11), kind=kOutput, calls=%fused_computation.8 | convolution fusion | flops 100675584 | bytes 7091712 | tf_op jit(solution)/shard_map/cvj,coj->cvo/dot_general | solution.py:51
  48.8 0.9 add_convert_fusion.1
  49.7 82.6 %all-gather.3.cloned.1.call-done = bf16[8192,1024]{1,0:T(8,128)(2,1)} async-done(((bf16[1024,1024]{1,0:T(8,128)(2,1)}), bf16[8192,1024]{1,0:T(8,128)(2,1)}) %all-gather.3.cloned.1.call-update) | async-done | bytes 16777232 | tf_op jit(solution)/shard_map/all_gather | solution.py:65
  132.3 12.1 %fusion.15 = f32[384,1024]{1,0:T(8,128)S(1)} fusion(bf16[384,8192]{1,0:T(8,128)(2,1)} %param.8, bf16[8192,1024]{1,0:T(8,128)(2,1)} %all-gather.3.cloned.1.call-done), kind=kOutput, calls=%fused_computation.41 | convolution fusion | flops 6442450944 | bytes 24641536 | tf_op jit(solution)/shard_map/dot_general | solution.py:66
  144.4 13.4 %fusion.16 = f32[384,8192]{1,0:T(8,128)} fusion(bf16[384,1024]{1,0:T(8,128)(2,1)S(1)} %copy-done, bf16[8192,1024]{1,0:T(8,128)(2,1)} %all-gather.3.cloned.1.call-done), kind=kOutput, calls=%fused_computation.42 | convolution fusion | flops 6442450944 | bytes 30146560 | tf_op jit(solution)/shard_map/dot_general | solution.py:67
  157.8 9.2 %multiply_convert_fusion = bf16[3,128,8192]{2,1,0:T(8,128)(2,1)} fusion(f32[3,128,8192]{2,1,0:T(8,128)} %bitcast.55, bf16[3,16,128]{2,1,0:T(8,128)(2,1)S(1)} %fusion.1, f32[3,128]{1,0:T(4,128)S(1)} %fusion.11, bf16[1,3,16,8192]{3,1,2,0:T(4,128)(2,1)S(1)} %bitcast.58), kind=kOutput, calls=%fused_computation.2 | convolution fusion | flops 110100480 | bytes 19674624 | tf_op jit(solution)/shard_map/uio,uof->uif/dot_general | solution.py:62
  167.0 1.3 multiply_convert_fusion.1
  168.3 9.2 %reduce-scatter.3.cloned.1.call-done = bf16[1,16,8192]{2,1,0:T(8,128)(2,1)} async-done(((bf16[8,16,8192]{2,1,0:T(8,128)(2,1)}), bf16[1,16,8192]{2,1,0:T(8,128)(2,1)}) %reduce-scatter.3.cloned.1.call-update) | async-done | bytes 262160 | tf_op jit(solution)/shard_map/reduce_scatter | solution.py:95
  177.4 37.4 %reduce-scatter.5.cloned.1.call-done = bf16[1,16,1024]{2,1,0:T(8,128)(2,1)} async-done(((bf16[8,16,1024]{2,1,0:T(8,128)(2,1)}), bf16[1,16,1024]{2,1,0:T(8,128)(2,1)}) %reduce-scatter.5.cloned.1.call-update) | async-done | bytes 32784 | tf_op jit(solution)/shard_map/reduce_scatter | solution.py:101
  (16 shorter events, 1.0 us)
Async XLA Ops:
  7.2 17.1 %copy-start = (bf16[384,1024]{1,0:T(8,128)(2,1)S(1)}, bf16[384,1024]{1,0:T(8,128)(2,1)}, u32[]{:S(2)}) copy-start(bf16[384,1024]{1,0:T(8,128)(2,1)} %param.9) | copy-start | bytes 2359300
  7.2 33.4 %all-gather.5.cloned.1.call-start = ((), (), s32[]{:S(2)}) async-start(), calls=%async_computation.3 | async-start | bytes 2359296 | tf_op jit(solution)/shard_map/all_gather | solution.py:36
  7.9 124.4 %all-gather.3.cloned.1.call-start = ((), (), s32[]{:S(2)}) async-start(), calls=%async_computation.2 | async-start | bytes 18874368 | tf_op jit(solution)/shard_map/all_gather | solution.py:65
  8.7 168.8 %reduce-scatter.3.cloned.1.call-start = ((), (), s32[]{:S(2)}) async-start(), calls=%async_computation.4 | async-start | bytes 2359296 | tf_op jit(solution)/shard_map/reduce_scatter | solution.py:95
  28.3 2.5 %copy-start.1 = (s32[3]{0:T(128)S(1)}, s32[3]{0:T(128)}, u32[]{:S(2)}) copy-start(s32[3]{0:T(128)} %param.14) | copy-start | bytes 40
  30.6 184.2 %reduce-scatter.5.cloned.1.call-start = ((), (), s32[]{:S(2)}) async-start(), calls=%async_computation.5 | async-start | bytes 294912 | tf_op jit(solution)/shard_map/reduce_scatter | solution.py:101
Sparse Core Ops, SparseCore 0:
  9.9 30.5 all-gather.4
  42.4 89.8 all-gather.2
  136.2 41.2 reduce-scatter.2
  181.2 33.5 reduce-scatter.4
where the time goes:
time: 222 us; the launch traced here: 221 us
  waiting for transfers between devices  140 us (63%)
  matrix products  45.8 us (21%)
  between operations  13.8 us (6%)
  blocking collectives  11 us (5%)
  other arithmetic  6.64 us (3%)
  local copies, waits for them, and re-layouts  3.62 us (2%)
    all_gather x1, waiting for transfers between devices, on_device(): lax.all_gather(frozen_value_weight, 'fsdp', axis=0, tiled=True)  82.6 us
    reduce_scatter x1, waiting for transfers between devices, on_device(): lax.psum_scatter(term_up.astype(jnp.float32).astype(jnp.bfloat16), 'fsdp'...  37.4 us
    dot_general x1, matrix products, on_device(): lax.dot_general(output_gradient, weight_piece, (((1,), (1,)), ((), ())),...  13.4 us
    dot_general x1, matrix products, on_device(): jnp.dot(tokens, weight_piece, preferred_element_type=jnp.float32)  12.1 us
    all_gather x1, blocking collectives, on_device(): lax.all_gather(adapter_up_maps, 'fsdp', axis=0, tiled=True)  11 us
    all_gather x1, waiting for transfers between devices, on_device(): lax.all_gather(adapter_down_maps, 'fsdp', axis=0, tiled=True)  9.62 us
    dot_general x1, matrix products, on_device(): jnp.einsum('uio,uof->uif', low_rank_gradient, down_block, preferred_eleme...  9.17 us
    reduce_scatter x1, waiting for transfers between devices, on_device(): lax.psum_scatter(term_down.astype(jnp.float32).astype(jnp.bfloat16), 'fsd...  9.16 us
  transfers between devices with their start and end apart: 4, of which 4 were waited for; matrix products, arithmetic and copies ran while one was open for 25% of the time, Pallas kernels for 0%

commit v1 on v0

--- a/solution.py
+++ b/solution.py
@@ -4,6 +4,27 @@
 from jax.sharding import PartitionSpec as P
 
 ADAPTER_SCALE = 2.0
+
+
+def ring_gather(x, axis, dim):
+    size, place, extent = (lax.axis_size(axis), lax.axis_index(axis), x.shape[dim])
+    right = [(i, (i + 1) % size) for i in range(size)]
+    downward = [(i, (i - 1) % size) for i in range(size)]
+    out = jnp.zeros((*x.shape[:dim], size * extent, *x.shape[dim + 1 :]), x.dtype)
+    out = lax.dynamic_update_slice_in_dim(out, x, place * extent, axis=dim)
+    from_left = from_right = x
+    half = size // 2
+    for lap in range(1, half + 1):
+        from_left = lax.ppermute(from_left, axis, right)
+        out = lax.dynamic_update_slice_in_dim(
+            out, from_left, (place - lap) % size * extent, axis=dim
+        )
+        if lap < size - half:
+            from_right = lax.ppermute(from_right, axis, downward)
+            out = lax.dynamic_update_slice_in_dim(
+                out, from_right, (place + lap) % size * extent, axis=dim
+            )
+    return out
 
 
 def on_device(
@@ -62,7 +83,7 @@
     adapter_backward = jnp.einsum(
         "uio,uof->uif", low_rank_gradient, down_block, preferred_element_type=jnp.float32
     )
-    weight_piece = lax.all_gather(frozen_value_weight, "fsdp", axis=0, tiled=True)
+    weight_piece = ring_gather(frozen_value_weight, "fsdp", 0)
     output_total = jnp.dot(tokens, weight_piece, preferred_element_type=jnp.float32)
     backward_piece = lax.dot_general(
         output_gradient, weight_piece, (((1,), (1,)), ((), ())), preferred_element_type=jnp.float32

time: 222 us -> 262 us (1.18)
  waiting for transfers between devices: 140 us -> 82.8 us
  blocking collectives: 11 us -> 58.2 us
  local copies, waits for them, and re-layouts: 3.62 us -> 31.5 us
  other arithmetic: 6.64 us -> 16.5 us
  starting transfers between devices: 0.34 us -> 9 us
  matrix products: 45.8 us -> 49.1 us
    ppermute x0 -> x7, waiting for transfers between devices: none -> 82.7 us  [the longest x4 70.9 us: ring_gather(): from_left = lax.ppermute(from_left, axis, right)]
    all_gather x1 -> x0, waiting for transfers between devices: 82.6 us -> none  [on_device(): lax.all_gather(frozen_value_weight, 'fsdp', axis=0, tiled=True)]
    all_gather x1, blocking collectives: 11 us -> 58.2 us  [on_device(): lax.all_gather(adapter_up_maps, 'fsdp', axis=0, tiled=True)]
    reduce_scatter x1, waiting for transfers between devices: 37.4 us -> 0.01 us  [on_device(): lax.psum_scatter(term_up.astype(jnp.float32).astype(jnp.bfloat16), 'fsdp'...]
    dynamic_update_slice x0 -> x8, local copies, waits for them, and re-layouts: none -> 21.9 us  [the longest x4 11 us: ring_gather(): lax.dynamic_update_slice_in_dim(out, from_left, (place - lap) % size * ex...]
    dot_general x1, matrix products: 13.4 us -> 24.6 us  [on_device(): lax.dot_general(output_gradient, weight_piece, (((1,), (1,)), ((), ())),...]
    convert_element_type x0 -> x2, other arithmetic: none -> 9.82 us  [the longest x1 8.69 us: on_device(): token_gradient.astype(jnp.bfloat16).reshape(tok_rows, model_width_size)]
    all_gather x1, waiting for transfers between devices: 9.62 us -> 0.01 us  [on_device(): lax.all_gather(adapter_down_maps, 'fsdp', axis=0, tiled=True)]
  transfers between devices with their start and end apart: 4 -> 10, of which waited for: 4 -> 4; matrix products, arithmetic and copies ran while one was open for 25% -> 37% of each run, Pallas kernels for 0% -> 0%
where the time goes in v1:
time: 262 us; the launch traced here: 261 us
  waiting for transfers between devices  82.8 us (32%)
  blocking collectives  58.2 us (22%)
  matrix products  49.1 us (19%)
  local copies, waits for them, and re-layouts  31.5 us (12%)
  other arithmetic  16.5 us (6%)
  between operations  13.9 us (5%)
  starting transfers between devices  9 us (3%)
    ppermute x4, waiting for transfers between devices, ring_gather(): from_left = lax.ppermute(from_left, axis, right)  70.9 us
    all_gather x1, blocking collectives, on_device(): lax.all_gather(adapter_up_maps, 'fsdp', axis=0, tiled=True)  58.2 us
    dot_general x1, matrix products, on_device(): lax.dot_general(output_gradient, weight_piece, (((1,), (1,)), ((), ())),...  24.6 us
    ppermute x3, waiting for transfers between devices, ring_gather(): from_right = lax.ppermute(from_right, axis, downward)  11.9 us
    dynamic_update_slice x4, local copies, waits for them, and re-layouts, ring_gather(): lax.dynamic_update_slice_in_dim(out, from_left, (place - lap) % size * ex...  11 us
    dot_general x1, matrix products, on_device(): jnp.dot(tokens, weight_piece, preferred_element_type=jnp.float32)  10.5 us
    dynamic_update_slice x3, local copies, waits for them, and re-layouts, ring_gather(): lax.dynamic_update_slice_in_dim(out, from_right, (place + lap) % size * e...  9.34 us
    convert_element_type x1, other arithmetic, on_device(): token_gradient.astype(jnp.bfloat16).reshape(tok_rows, model_width_size)  8.69 us
  transfers between devices with their start and end apart: 10, of which 4 were waited for; matrix products, arithmetic and copies ran while one was open for 37% of the time, Pallas kernels for 0%

profile of v1, /device:TPU:0, one launch (start us, length us, event | category | flops | bytes accessed | tf_op | source)
XLA Modules:
  0.0 261.1 jit_solution(792765522471908547)
XLA Ops:
  7.7 2.9 %collective-permute-start.1 = (bf16[1024,1024]{1,0:T(8,128)(2,1)}, bf16[1024,1024]{1,0:T(8,128)(2,1)}, u32[]{:S(2)}, u32[]{:S(2)}) collective-permute-start(bf16[1024,1024]{1,0:T(8,128)(2,1)} %param.10), channel_id=1, source_target_pairs={{0,28},{4,0},{8,4},{12,8},{16,12},{20,16},{24,20},{28,24},{1,29},{... | collective-permute-start | bytes 6291464 | tf_op jit(solution)/shard_map/ppermute | solution.py:23
  11.6 58.2 %all_gather.7 = bf16[8,16,1024]{2,1,0:T(8,128)(2,1)S(1)} all-gather(bf16[1,16,1024]{2,1,0:T(8,128)(2,1)} %param.12), channel_id=1, replica_groups=mesh['fsdp'=8,'dp'=4] {'fsdp'}, dimensions={0}, use_global_device_ids=true | all-gather | bytes 294912 | tf_op jit(solution)/shard_map/all_gather | solution.py:58
  71.3 3.7 %fusion.18 = f32[3,16,8192]{2,1,0:T(8,128)S(1)} fusion(bf16[3,16,128]{2,1,0:T(8,128)(2,1)S(1)} %fusion.1, bf16[3,128,8192]{2,1,0:T(8,128)(2,1)} %bitcast.57), kind=kOutput, calls=%fused_computation.52 | convolution fusion | flops 100663296 | bytes 7876608 | tf_op jit(solution)/shard_map/vio,vih->voh/dot_general | solution.py:100
  78.2 2.3 collective-permute-start.3
  80.5 2.2 add_convert_fusion
  82.7 51.2 %collective-permute-done.2 = bf16[1024,1024]{1,0:T(8,128)(2,1)} collective-permute-done((bf16[1024,1024]{1,0:T(8,128)(2,1)S(1)}, bf16[1024,1024]{1,0:T(8,128)(2,1)}, u32[]{:S(2)}, u32[]{:S(2)}) %collective-permute-start.2) | collective-permute-done | bytes 2097184 | tf_op jit(solution)/shard_map/ppermute | solution.py:18
  133.9 6.0 %broadcast_in_dim.14 = bf16[8192,1024]{1,0:T(8,128)(2,1)} broadcast(bf16[]{:T(256)} %constant.64.clone.1), dimensions={} | broadcast | bytes 16777218 | tf_op jit(solution)/shard_map/broadcast_in_dim | solution.py:13
  139.9 1.5 constant_dynamic-update-slice_fusion.7
  143.0 3.1 %constant_dynamic-update-slice_fusion.5 = bf16[8192,1024]{1,0:T(8,128)(2,1)} fusion(bf16[8192,1024]{1,0:T(8,128)(2,1)} %constant_dynamic-update-slice_fusion.6, bf16[1024,1024]{1,0:T(8,128)(2,1)} %collective-permute-done.1, s32[]{:T(128)S(6)} %select_n.72), kind=kLoop, calls=%fused_computation.35 | loop fusion | bytes 4194308 | tf_op jit(solution)/shard_map/dynamic_update_slice | solution.py:24
  146.1 2.8 %copy.12 = bf16[1,8,16,8192]{3,1,2,0:T(8,128)(2,1)S(1)} copy(bf16[1,8,16,8192]{3,2,1,0:T(8,128)(2,1)} %bitcast.66) | data formatting | bytes 4194304
  149.6 2.7 %collective-permute-start.5 = (bf16[1024,1024]{1,0:T(8,128)(2,1)}, bf16[1024,1024]{1,0:T(8,128)(2,1)}, u32[]{:S(2)}, u32[]{:S(2)}) collective-permute-start(bf16[1024,1024]{1,0:T(8,128)(2,1)} %collective-permute-done.3), channel_id=1, source_target_pairs={{0,28},{4,0},{8,4},{12,8},{16,12},{20,16},{24,20},{28,24},{1,29},{... | collective-permute-start | bytes 6291464 | tf_op jit(solution)/shard_map/ppermute | solution.py:23
  152.3 5.1 %fusion = bf16[3,16,128]{2,1,0:T(8,128)(2,1)} fusion(bf16[3,128,8192]{2,1,0:T(8,128)(2,1)} %bitcast.58, bf16[1,3,16,8192]{3,1,2,0:T(4,128)(2,1)S(1)} %bitcast.63, f32[3,128]{1,0:T(4,128)S(1)} %fusion.13), kind=kOutput, calls=%fused_computation.8 | convolution fusion | flops 100675584 | bytes 7091712 | tf_op jit(solution)/shard_map/cvj,coj->cvo/dot_general | solution.py:72
  157.4 12.6 %collective-permute-done.4 = bf16[1024,1024]{1,0:T(8,128)(2,1)} collective-permute-done((bf16[1024,1024]{1,0:T(8,128)(2,1)}, bf16[1024,1024]{1,0:T(8,128)(2,1)}, u32[]{:S(2)}, u32[]{:S(2)}) %collective-permute-start.4) | collective-permute-done | bytes 2097184 | tf_op jit(solution)/shard_map/ppermute | solution.py:18
  173.0 1.8 fusion.2
  174.8 3.1 %constant_dynamic-update-slice_fusion.4 = bf16[8192,1024]{1,0:T(8,128)(2,1)} fusion(bf16[8192,1024]{1,0:T(8,128)(2,1)} %constant_dynamic-update-slice_fusion.5, bf16[1024,1024]{1,0:T(8,128)(2,1)} %collective-permute-done.2, s32[]{:T(128)S(6)} %select_n.74), kind=kLoop, calls=%fused_computation.34 | loop fusion | bytes 4194308 | tf_op jit(solution)/shard_map/dynamic_update_slice | solution.py:19
  177.9 3.1 %constant_dynamic-update-slice_fusion.3 = bf16[8192,1024]{1,0:T(8,128)(2,1)} fusion(bf16[8192,1024]{1,0:T(8,128)(2,1)} %constant_dynamic-update-slice_fusion.4, bf16[1024,1024]{1,0:T(8,128)(2,1)} %collective-permute-done.3, s32[]{:T(128)S(6)} %select_n.76), kind=kLoop, calls=%fused_computation.33 | loop fusion | bytes 4194308 | tf_op jit(solution)/shard_map/dynamic_update_slice | solution.py:24
  181.1 3.1 %constant_dynamic-update-slice_fusion.2 = bf16[8192,1024]{1,0:T(8,128)(2,1)} fusion(bf16[8192,1024]{1,0:T(8,128)(2,1)} %constant_dynamic-update-slice_fusion.3, bf16[1024,1024]{1,0:T(8,128)(2,1)} %collective-permute-done.4, s32[]{:T(128)S(6)} %select_n.78), kind=kLoop, calls=%fused_computation.32 | loop fusion | bytes 4194308 | tf_op jit(solution)/shard_map/dynamic_update_slice | solution.py:19
  184.2 11.8 %collective-permute-done.5 = bf16[1024,1024]{1,0:T(8,128)(2,1)} collective-permute-done((bf16[1024,1024]{1,0:T(8,128)(2,1)}, bf16[1024,1024]{1,0:T(8,128)(2,1)}, u32[]{:S(2)}, u32[]{:S(2)}) %collective-permute-start.5) | collective-permute-done | bytes 2097184 | tf_op jit(solution)/shard_map/ppermute | solution.py:23
  196.1 3.1 %constant_dynamic-update-slice_fusion.1 = bf16[8192,1024]{1,0:T(8,128)(2,1)} fusion(bf16[8192,1024]{1,0:T(8,128)(2,1)} %constant_dynamic-update-slice_fusion.2, bf16[1024,1024]{1,0:T(8,128)(2,1)} %collective-permute-done.5, s32[]{:T(128)S(6)} %select_n.80), kind=kLoop, calls=%fused_computation.31 | loop fusion | bytes 4194308 | tf_op jit(solution)/shard_map/dynamic_update_slice | solution.py:24
  199.2 7.1 %collective-permute-done.6 = bf16[1024,1024]{1,0:T(8,128)(2,1)} collective-permute-done((bf16[1024,1024]{1,0:T(8,128)(2,1)}, bf16[1024,1024]{1,0:T(8,128)(2,1)}, u32[]{:S(2)}, u32[]{:S(2)}) %collective-permute-start.6) | collective-permute-done | bytes 2097184 | tf_op jit(solution)/shard_map/ppermute | solution.py:18
  206.3 3.3 %constant_dynamic-update-slice_fusion = bf16[8192,1024]{1,0:T(8,128)(2,1)} fusion(bf16[8192,1024]{1,0:T(8,128)(2,1)} %constant_dynamic-update-slice_fusion.1, bf16[1024,1024]{1,0:T(8,128)(2,1)} %collective-permute-done.6, s32[]{:T(128)S(6)} %select_n.82), kind=kLoop, calls=%fused_computation.30 | loop fusion | bytes 4194308 | tf_op jit(solution)/shard_map/dynamic_update_slice | solution.py:19
  209.6 24.6 %fusion.17 = f32[8192,384]{0,1:T(8,128)} fusion(bf16[8192,1024]{1,0:T(8,128)(2,1)} %constant_dynamic-update-slice_fusion, bf16[384,1024]{1,0:T(8,128)(2,1)S(1)} %copy-done), kind=kOutput, calls=%fused_computation.51 | convolution fusion | flops 6442450944 | bytes 30146560 | tf_op jit(solution)/shard_map/dot_general | solution.py:88
  234.2 8.7 %multiply_convert_fusion = bf16[3,128,8192]{2,1,0:T(8,128)(2,1)} fusion(f32[3,128,8192]{2,1,0:T(8,128)} %bitcast.61, f32[3,128,8192]{2,1,0:T(8,128)S(1)} %fusion.2, f32[3,128]{1,0:T(4,128)S(1)} %fusion.13), kind=kLoop, calls=%fused_computation.2 | loop fusion | flops 9437184 | bytes 31458816 | tf_op jit(solution)/shard_map/convert_element_type | solution.py:99
  242.9 10.5 %fusion.19 = f32[1024,384]{0,1:T(8,128)S(1)} fusion(bf16[384,8192]{1,0:T(8,128)(2,1)S(1)} %bitcast.60, bf16[8192,1024]{1,0:T(8,128)(2,1)} %constant_dynamic-update-slice_fusion), kind=kOutput, calls=%fused_computation.53 | convolution fusion | flops 6442450944 | bytes 24641536 | tf_op jit(solution)/shard_map/dot_general | solution.py:87
  (47 shorter events, 12.5 us)
Async XLA Ops:
  7.2 63.9 %copy-start = (bf16[384,1024]{1,0:T(8,128)(2,1)S(1)}, bf16[384,1024]{1,0:T(8,128)(2,1)}, u32[]{:S(2)}) copy-start(bf16[384,1024]{1,0:T(8,128)(2,1)} %param.9) | copy-start | bytes 2359300
  7.2 138.9 %all-gather.2.cloned.1.call-start = ((), (), s32[]{:S(2)}) async-start(), calls=%async_computation.2 | async-start | bytes 2359296 | tf_op jit(solution)/shard_map/all_gather | solution.py:57
  7.2 70.5 %collective-permute-start = (bf16[1024,1024]{1,0:T(8,128)(2,1)}, bf16[1024,1024]{1,0:T(8,128)(2,1)S(1)}, u32[]{:S(2)}, u32[]{:S(2)}) collective-permute-start(bf16[1024,1024]{1,0:T(8,128)(2,1)} %param.10), channel_id=1, source_target_pairs={{0,4},{4,8},{8,12},{12,16},{16,20},{20,24},{24,28},{28,0},{1,5},{5... | collective-permute-start | bytes 6291464 | tf_op jit(solution)/shard_map/ppermute | solution.py:18
  7.7 70.4 %collective-permute-start.1 = (bf16[1024,1024]{1,0:T(8,128)(2,1)}, bf16[1024,1024]{1,0:T(8,128)(2,1)}, u32[]{:S(2)}, u32[]{:S(2)}) collective-permute-start(bf16[1024,1024]{1,0:T(8,128)(2,1)} %param.10), channel_id=1, source_target_pairs={{0,28},{4,0},{8,4},{12,8},{16,12},{20,16},{24,20},{28,24},{1,29},{... | collective-permute-start | bytes 6291464 | tf_op jit(solution)/shard_map/ppermute | solution.py:23
  10.7 243.8 %reduce-scatter.3.cloned.1.call-start = ((), (), s32[]{:S(2)}) async-start(), calls=%async_computation.3 | async-start | bytes 2359296 | tf_op jit(solution)/shard_map/reduce_scatter | solution.py:116
  77.8 56.2 %collective-permute-start.2 = (bf16[1024,1024]{1,0:T(8,128)(2,1)S(1)}, bf16[1024,1024]{1,0:T(8,128)(2,1)}, u32[]{:S(2)}, u32[]{:S(2)}) collective-permute-start(bf16[1024,1024]{1,0:T(8,128)(2,1)S(1)} %collective-permute-done), channel_id=1, source_target_pairs={{0,4},{4,8},{8,12},{12,16},{16,20},{20,24},{24,28},{28,0},{1,5},{5... | collective-permute-start | bytes 6291464 | tf_op jit(solution)/shard_map/ppermute | solution.py:18
  78.2 71.4 %collective-permute-start.3 = (bf16[1024,1024]{1,0:T(8,128)(2,1)}, bf16[1024,1024]{1,0:T(8,128)(2,1)}, u32[]{:S(2)}, u32[]{:S(2)}) collective-permute-start(bf16[1024,1024]{1,0:T(8,128)(2,1)} %collective-permute-done.1), channel_id=1, source_target_pairs={{0,28},{4,0},{8,4},{12,8},{16,12},{20,16},{24,20},{28,24},{1,29},{... | collective-permute-start | bytes 6291464 | tf_op jit(solution)/shard_map/ppermute | solution.py:23
  82.7 171.9 %reduce-scatter.5.cloned.1.call-start = ((), (), s32[]{:S(2)}) async-start(), calls=%async_computation.4 | async-start | bytes 294912 | tf_op jit(solution)/shard_map/reduce_scatter | solution.py:122
  133.9 36.1 %collective-permute-start.4 = (bf16[1024,1024]{1,0:T(8,128)(2,1)}, bf16[1024,1024]{1,0:T(8,128)(2,1)}, u32[]{:S(2)}, u32[]{:S(2)}) collective-permute-start(bf16[1024,1024]{1,0:T(8,128)(2,1)} %collective-permute-done.2), channel_id=1, source_target_pairs={{0,4},{4,8},{8,12},{12,16},{16,20},{20,24},{24,28},{28,0},{1,5},{5... | collective-permute-start | bytes 6291464 | tf_op jit(solution)/shard_map/ppermute | solution.py:18
  133.9 6.0 %copy-start.2 = (bf16[1024,1024]{1,0:T(8,128)(2,1)S(1)}, bf16[1024,1024]{1,0:T(8,128)(2,1)}, u32[]{:S(2)}) copy-start(bf16[1024,1024]{1,0:T(8,128)(2,1)} %param.10) | copy-start | bytes 6291460
  133.9 7.5 %copy-start.3 = (s32[3]{0:T(128)S(1)}, s32[3]{0:T(128)}, u32[]{:S(2)}) copy-start(s32[3]{0:T(128)} %param.14) | copy-start | bytes 40
  149.6 46.5 %collective-permute-start.5 = (bf16[1024,1024]{1,0:T(8,128)(2,1)}, bf16[1024,1024]{1,0:T(8,128)(2,1)}, u32[]{:S(2)}, u32[]{:S(2)}) collective-permute-start(bf16[1024,1024]{1,0:T(8,128)(2,1)} %collective-permute-done.3), channel_id=1, source_target_pairs={{0,28},{4,0},{8,4},{12,8},{16,12},{20,16},{24,20},{28,24},{1,29},{... | collective-permute-start | bytes 6291464 | tf_op jit(solution)/shard_map/ppermute | solution.py:23
  170.0 36.3 %collective-permute-start.6 = (bf16[1024,1024]{1,0:T(8,128)(2,1)}, bf16[1024,1024]{1,0:T(8,128)(2,1)}, u32[]{:S(2)}, u32[]{:S(2)}) collective-permute-start(bf16[1024,1024]{1,0:T(8,128)(2,1)} %collective-permute-done.4), channel_id=1, source_target_pairs={{0,4},{4,8},{8,12},{12,16},{16,20},{20,24},{24,28},{28,0},{1,5},{5... | collective-permute-start | bytes 6291464 | tf_op jit(solution)/shard_map/ppermute | solution.py:18
  206.3 36.6 %slice-start = ((s8[6291456]{0:T(1024)(128)(4,1)}), s8[4194304]{0:T(1024)(128)(4,1)S(1)}, s32[]{:S(2)}) async-start(s8[6291456]{0:T(1024)(128)(4,1)} %bitcast.59), calls=%async_computation.5 | async-start | bytes 8388608
  209.6 33.3 %slice-start.1 = ((s8[6291456]{0:T(1024)(128)(4,1)}), s8[2097152]{0:T(1024)(128)(4,1)S(1)}, s32[]{:S(2)}) async-start(s8[6291456]{0:T(1024)(128)(4,1)} %bitcast.59), calls=%async_computation.6 | async-start | bytes 4194304
  242.9 11.7 %copy-start.1 = (bf16[384,1024]{1,0:T(8,128)(2,1)S(1)}, bf16[384,1024]{1,0:T(8,128)(2,1)}, u32[]{:S(2)}) copy-start(bf16[384,1024]{1,0:T(8,128)(2,1)} %param.9) | copy-start | bytes 2359300
Sparse Core Ops, SparseCore 0:
  10.8 38.1 all-gather.1
  82.8 50.4 reduce-scatter.2
  172.0 35.8 reduce-scatter.4
